TPU v7x, 128 devices: a whole 4x4x4 slice. The times are simulated.
128 devices in a mesh: half: 2 (over core), row: 8 (over z_hi, x), col: 8 (over y, z_lo).
Axes of the slice: x: 4, y: 4, z: 4 (z_hi: 2, z_lo: 2; z = z_hi * 2 + z_lo), core: 2. Of those that a mesh axis runs over, the one named last changes fastest.
Arguments:
- child_diag: float32 [2, 512, 512], P('half'), as said below
- child_panel: float32 [2, 16, 8, 128, 512], P('half', None, 'row'), may hold values from -18 to 18
- child_window: float32 [2, 16, 8, 128, 8, 8, 128], P('half', None, 'row', None, None, 'col'), may hold values from -6 to 6
- parent_diag: float32 [512, 512], replicated
- parent_lead_panel: float32 [24, 8, 2, 8, 8, 512], P(None, 'row', 'half', 'col'), may hold values from -24 to 24
- index_maps: int32 [2, 128], replicated, may hold values from 0 to 191, as said below
Outputs:
- parent_front: float32 [24, 8, 128, 4, 2, 8, 128], P(None, 'row', None, None, 'half', 'col')
- parent_factor: float32 [24, 8, 2, 8, 8, 512], P(None, 'row', 'half', 'col')
- parent_pivot: float32 [512, 512], replicated
Inputs may be any that keep to these rules, and one draw needn't show every extreme that they name: child_diag and parent_diag are symmetric and positive definite. For each child k and each group a, the entries index_maps[k, a * 16 + u] with 0 <= u < 16 equal q * 16 + ((u + s) mod 16) for a group target q and a turn s fixed within the group; groups a < 4 have q = a, later groups have distinct q that rise with a; over the 8 groups of a child the turns s, taken modulo 8, are all different; for each child some group a < 4 has a turn divisible by 8, and another group a < 4 has a turn that leaves 1 modulo 8.
All inputs are finite; a program needn't handle non-finite values.
Results may differ from a plain program's by a relative error of at most 0.0001.
Values sent between devices are 32-bit elements; how exact they have to be, the bound alone decides.
No kernel may reach another device: no remote copies, remote signals or barrier semaphores. Data moves between devices by JAX's collectives and lax.ppermute only.
A program may use at most 192 MiB of HBM per device.

v0:
```python
import jax
import jax.numpy as jnp
from jax import lax
from jax.sharding import PartitionSpec as P

BLOCK_EXTENT = 128
PB = 4
SB = 128
RB = 192
WB = 64


def from_root(shard, axis, root):
    mine = lax.axis_index(axis) == root
    return lax.psum(jnp.where(mine, shard, jnp.zeros_like(shard)), axis)


def pick_ranked(owners, values, wanted, slot_count, missing):
    matches = owners[..., None, :] == wanted[:, None]
    ranking = jnp.cumsum(matches.astype(jnp.int32), axis=-1) - 1
    slot_ids = jnp.arange(slot_count, dtype=jnp.int32)
    chosen = matches[..., None, :] & (ranking[..., None, :] == slot_ids[:, None])
    present = jnp.any(chosen, axis=-1)
    picked = jnp.sum(jnp.where(chosen, values[..., None, None, :], 0), axis=-1)
    return jnp.where(present, picked, missing)


def per_device(child_diag, child_panel, child_window, parent_diag, parent_lead_panel, index_maps):
    highest = lax.Precision.HIGHEST
    row_size = lax.axis_size("row")
    half_id = lax.axis_index("half")
    row_id = lax.axis_index("row")
    col_id = lax.axis_index("col")
    panel_width = PB * BLOCK_EXTENT
    group_size = 2 * row_size
    row_local = SB // row_size
    col_local = WB // row_size
    parent_row_blocks = RB // row_size
    parent_cols = WB // group_size
    per_row = 2 * (SB // group_size) // row_size
    per_col = (WB // group_size + row_size - 1) // row_size
    pivot_lower_factor = jnp.linalg.cholesky(parent_diag)
    own_rows = parent_lead_panel.reshape(-1, panel_width)
    solved = jax.scipy.linalg.solve_triangular(pivot_lower_factor, own_rows.T, lower=True).T
    parent_factor = solved.reshape(parent_lead_panel.shape)
    sub_rows = parent_lead_panel.shape[4]
    gathered = lax.all_gather(
        solved.reshape(parent_row_blocks, sub_rows, panel_width),
        ("half", "col"),
        axis=1,
        tiled=True,
    )
    paired = gathered[: 2 * parent_cols].reshape(parent_cols, 2, BLOCK_EXTENT, panel_width)
    offered = lax.dynamic_index_in_dim(paired, half_id, axis=1, keepdims=False)
    column_factor = from_root(offered, "row", col_id)
    child_low = jnp.linalg.cholesky(child_diag[0])
    child_rows = child_panel.reshape(-1, panel_width)
    child_factor = jax.scipy.linalg.solve_triangular(child_low, child_rows.T, lower=True).T
    leading = child_factor[: col_local * BLOCK_EXTENT]
    everyone = lax.all_gather(leading[None], "row", axis=0, tiled=True)
    child_columns = lax.dynamic_index_in_dim(everyone, col_id, axis=0, keepdims=False)
    schur_part = child_window.reshape(row_local * BLOCK_EXTENT, col_local * BLOCK_EXTENT) - jnp.dot(
        child_factor, child_columns.T, precision=highest
    )
    schur_blocks = schur_part.reshape(row_local, BLOCK_EXTENT, col_local, BLOCK_EXTENT)
    child_map = lax.dynamic_index_in_dim(index_maps, half_id, axis=0, keepdims=False)
    my_rows = lax.dynamic_index_in_dim(
        child_map.reshape(row_local, row_size), row_id, axis=1, keepdims=False
    )
    my_cols = lax.dynamic_index_in_dim(
        child_map[:WB].reshape(col_local, row_size), col_id, axis=1, keepdims=False
    )
    local_rows = jnp.arange(row_local, dtype=jnp.int32)
    local_cols = jnp.arange(col_local, dtype=jnp.int32)
    send_rows = pick_ranked(
        my_rows % row_size, local_rows, jnp.arange(row_size, dtype=jnp.int32), per_row, row_local
    )
    send_cols = pick_ranked(
        my_cols % group_size,
        local_cols,
        jnp.arange(group_size, dtype=jnp.int32),
        per_col,
        col_local,
    )
    all_rows = index_maps.reshape(2, row_local, row_size).transpose(0, 2, 1)
    row_target = pick_ranked(
        all_rows % row_size, all_rows // row_size, row_id[None], per_row, parent_row_blocks
    )[:, :, 0, :]
    all_cols = index_maps[:, :WB].reshape(2, col_local, row_size).transpose(0, 2, 1)
    col_target = pick_ranked(
        all_cols % group_size,
        all_cols // group_size,
        (half_id * row_size + col_id)[None],
        per_col,
        parent_cols,
    )[:, :, 0, :]
    assembled_front = jnp.zeros(
        (parent_row_blocks, BLOCK_EXTENT, parent_cols, BLOCK_EXTENT), jnp.float32
    )
    row_index = send_rows[None, :, None, :, None]
    col_index = send_cols.reshape(2, row_size, per_col)[:, None, :, None, :]
    outgoing = schur_blocks.at[row_index, :, col_index, :].get(mode="fill", fill_value=0.0)
    arrived = lax.all_to_all(
        outgoing.reshape(-1, per_row * per_col, BLOCK_EXTENT, BLOCK_EXTENT),
        ("half", "row", "col"),
        split_axis=0,
        concat_axis=0,
        tiled=True,
    )
    arrived = arrived.reshape(2, row_size, row_size, per_row, per_col, BLOCK_EXTENT, BLOCK_EXTENT)
    target_rows = row_target[:, :, None, :, None]
    target_cols = col_target[:, None, :, None, :]
    assembled_front = assembled_front.at[target_rows, :, target_cols, :].add(arrived, mode="drop")
    flat_front = assembled_front.reshape(
        parent_row_blocks * BLOCK_EXTENT, parent_cols * BLOCK_EXTENT
    )
    updated = flat_front - jnp.dot(
        gathered.reshape(-1, panel_width),
        column_factor.reshape(-1, panel_width).T,
        precision=highest,
    )
    return (
        updated.reshape(parent_row_blocks, 1, BLOCK_EXTENT, parent_cols, 1, 1, BLOCK_EXTENT),
        parent_factor,
        pivot_lower_factor,
    )


def solution(mesh):
    in_specs = (
        P("half", None, None),
        P("half", None, "row", None, None),
        P("half", None, "row", None, None, "col", None),
        P(),
        P(None, "row", "half", "col", None, None),
        P(),
    )
    out_specs = (
        P(None, "row", None, None, "half", "col", None),
        P(None, "row", "half", "col", None, None),
        P(),
    )
    return jax.shard_map(
        per_device, mesh=mesh, in_specs=in_specs, out_specs=out_specs, check_vma=False
    )
```

profile of v0, /device:TPU:0, one launch (start us, length us, event | category | flops | bytes accessed | tf_op | source)
XLA Modules:
  0.0 819.9 jit_solution(16038382859682363218)
XLA Ops:
  14.1 11.7 %cholesky.286 = f32[128,128]{1,0:T(8,128)S(1)} custom-call(f32[128,128]{1,0:T(8,128)S(1)} %cholesky.426), custom_call_target="Cholesky" | custom-call | tf_op jit(solution)/shard_map/jit(cholesky)/cholesky | solution.py:56
  26.0 9.8 %custom-call.37 = f32[1,128,128]{1,2,0:T(8,128)S(1)} custom-call(f32[1,128,128]{2,1,0:T(8,128)S(1)} %get-tuple-element.91), custom_call_target="InvertDiagBlocksLowerTriangular" | custom-call | tf_op jit(solution)/shard_map/jit(cholesky)/cholesky | solution.py:56
  36.5 11.7 %cholesky.305 = f32[128,128]{1,0:T(8,128)S(1)} custom-call(f32[128,128]{1,0:T(8,128)S(1)} %cholesky.430), custom_call_target="Cholesky" | custom-call | tf_op jit(solution)/shard_map/jit(cholesky)/cholesky | solution.py:56
  48.2 10.2 %custom-call.38 = f32[1,128,128]{1,2,0:T(8,128)S(1)} custom-call(f32[1,128,128]{2,1,0:T(8,128)S(1)} %get-tuple-element.88), custom_call_target="InvertDiagBlocksLowerTriangular" | custom-call | tf_op jit(solution)/shard_map/jit(cholesky)/cholesky | solution.py:56
  59.1 11.7 %cholesky.326 = f32[128,128]{1,0:T(8,128)S(1)} custom-call(f32[128,128]{1,0:T(8,128)S(1)} %cholesky.435), custom_call_target="Cholesky" | custom-call | tf_op jit(solution)/shard_map/jit(cholesky)/cholesky | solution.py:56
  70.9 9.8 %custom-call.39 = f32[1,128,128]{1,2,0:T(8,128)S(1)} custom-call(f32[1,128,128]{2,1,0:T(8,128)S(1)} %get-tuple-element.85), custom_call_target="InvertDiagBlocksLowerTriangular" | custom-call | tf_op jit(solution)/shard_map/jit(cholesky)/cholesky | solution.py:56
  81.3 11.7 %cholesky.343 = f32[128,128]{1,0:T(8,128)S(1)} custom-call(f32[128,128]{1,0:T(8,128)S(1)} %convolution_subtract_fusion.10), custom_call_target="Cholesky" | custom-call | tf_op jit(solution)/shard_map/jit(cholesky)/cholesky | solution.py:56
  106.4 39.3 %custom-call.28 = f32[4,128,128]{1,2,0:T(8,128)S(1)} custom-call(f32[4,128,128]{2,1,0:T(8,128)S(1)} %get-tuple-element.11), custom_call_target="InvertDiagBlocksLowerTriangular" | custom-call | tf_op jit(solution)/shard_map/jit(_solve_triangular)/triangular_solve | solution.py:58
  169.6 11.9 %cholesky.358 = f32[128,128]{1,0:T(8,128)S(1)} custom-call(f32[128,128]{1,0:T(8,128)S(1)} %cholesky.439), custom_call_target="Cholesky" | custom-call | tf_op jit(solution)/shard_map/jit(cholesky)/cholesky | solution.py:42
  195.7 11.7 %cholesky.377 = f32[128,128]{1,0:T(8,128)S(1)} custom-call(f32[128,128]{1,0:T(8,128)S(1)} %cholesky.443), custom_call_target="Cholesky" | custom-call | tf_op jit(solution)/shard_map/jit(cholesky)/cholesky | solution.py:42
  208.1 9.8 %custom-call.41 = f32[1,128,128]{1,2,0:T(8,128)S(1)} custom-call(f32[1,128,128]{2,1,0:T(8,128)S(1)} %get-tuple-element.78), custom_call_target="InvertDiagBlocksLowerTriangular" | custom-call | tf_op jit(solution)/shard_map/jit(cholesky)/cholesky | solution.py:42
  220.2 12.1 %cholesky.398 = f32[128,128]{1,0:T(8,128)S(1)} custom-call(f32[128,128]{1,0:T(8,128)S(1)} %cholesky.448), custom_call_target="Cholesky" | custom-call | tf_op jit(solution)/shard_map/jit(cholesky)/cholesky | solution.py:42
  245.1 11.7 %cholesky.415 = f32[128,128]{1,0:T(8,128)S(1)} custom-call(f32[128,128]{1,0:T(8,128)S(1)} %convolution_subtract_fusion.9), custom_call_target="Cholesky" | custom-call | tf_op jit(solution)/shard_map/jit(cholesky)/cholesky | solution.py:42
  260.6 89.0 %all-gather.6.cloned.1.call-done = f32[8192,512]{0,1:T(8,128)} async-done(((f32[1024,512]{0,1:T(8,128)}), f32[8192,512]{0,1:T(8,128)}) %all-gather.6.cloned.1.call-update) | async-done | bytes 16777232 | tf_op jit(solution)/shard_map/all_gather | solution.py:60
  349.5 21.3 %copy.78 = f32[64,8,8,1024]{3,2,1,0:T(8,128)} copy(f32[64,8,8,1024]{3,1,2,0:T(8,128)} %bitcast.224) | data formatting | bytes 33554432
  380.3 20.5 %fusion = f32[256,8,8,128]{3,1,2,0:T(8,128)S(1)} fusion(f32[256,8,8,128]{3,2,1,0:T(8,128)} %bitcast.231, f32[128,2048]{1,0:T(8,128)} %copy-done.1, f32[128,2048]{1,0:T(8,128)S(1)} %fusion.56, f32[128,2048]{1,0:T(8,128)S(1)} %fusion.58, f32[128,2048]{1,0:T(8,128)S(1)} %fusion.16, f32[1,1024,512]{1,0,2:T(1,128)} %constant_dynamic-slice_fusion.2), kind=kOutput, calls=%fused_computation.7 | convolution fusion | flops 12890144768 | bytes 23068672 | tf_op jit(solution)/shard_map/dot_general | solution.py:62
  407.6 16.0 %gather_fusion = f32[256,128,128]{2,1,0:T(8,128)} fusion(f32[16,128,8,128]{3,1,2,0:T(8,128)} %copy.67, s32[256]{0:T(256)S(1)} %reshape.575), kind=kCustom, calls=%fused_computation | custom fusion | bytes 33556480 | tf_op jit(solution)/shard_map/gather | solution.py:102
  423.6 11.4 %broadcast_select_fusion = f32[128,2,128,128]{3,2,1,0:T(8,128)} fusion(f32[128,2,128,128]{3,2,1,0:T(8,128)} %bitcast.220, pred[128,2]{1,0:T(8,128)(4,1)S(1)} %bitcast.239), kind=kLoop, calls=%fused_computation.8 | loop fusion | flops 4194304 | bytes 33554688 | tf_op jit(solution)/shard_map/select_n | solution.py:102
  453.0 39.3 %custom-call.29 = f32[4,128,128]{1,2,0:T(8,128)S(1)} custom-call(f32[4,128,128]{2,1,0:T(8,128)S(1)} %get-tuple-element.19), custom_call_target="InvertDiagBlocksLowerTriangular" | custom-call | tf_op jit(solution)/shard_map/jit(_solve_triangular)/triangular_solve | solution.py:44
  495.5 205.3 %all-gather.4.cloned.1.call-done = f32[24,128,512]{2,1,0:T(8,128)} async-done(((f32[24,8,512]{2,1,0:T(8,128)}), f32[24,128,512]{2,1,0:T(8,128)}) %all-gather.4.cloned.1.call-update) | async-done | bytes 6291472 | tf_op jit(solution)/shard_map/all_gather | solution.py:47
  708.1 51.8 %scatter_fusion = f32[24,128,4,128]{3,1,2,0:T(8,128)} fusion(f32[24,128,4,128]{3,1,2,0:T(8,128)} %broadcast_in_dim.109, s32[256]{0:T(256)S(1)} %reshape.583, f32[256,128,128]{2,1,0:T(8,128)} %bitcast.23), kind=kCustom, calls=%fused_computation.1 | custom fusion | flops 4194304 | bytes 50333696 | tf_op jit(solution)/shard_map/scatter-add | solution.py:113
  759.9 10.5 %copy.68 = f32[24,128,4,128]{3,2,1,0:T(4,128)} copy(f32[24,128,4,128]{3,1,2,0:T(8,128)} %scatter_fusion) | data formatting | bytes 12582912 | tf_op jit(solution)/shard_map/scatter-add | solution.py:113
  770.4 18.2 %all-reduce.3.cloned.1.call-done = f32[512,512]{1,0:T(8,128)} async-done(((f32[512,512]{1,0:T(8,128)}), f32[512,512]{1,0:T(8,128)}) %all-reduce.3.cloned.1.call-update) | async-done | bytes 1048592 | tf_op jit(solution)/shard_map/psum | solution.py:15
  788.6 16.1 %bitcast_subtract_fusion.1 = f32[3072,512]{1,0:T(8,128)} fusion(f32[384,8,4,128]{3,2,1,0:T(4,128)} %bitcast.222, f32[3072,512]{1,0:T(8,128)} %bitcast.229, f32[512,512]{1,0:T(8,128)} %all-reduce.3.cloned.1.call-done), kind=kOutput, calls=%fused_computation.9 | convolution fusion | flops 9665249280 | bytes 19922944 | tf_op jit(solution)/shard_map/dot_general | solution.py:117
  (173 shorter events, 142.2 us)
Async XLA Ops:
  8.0 341.5 %all-gather.6.cloned.1.call-start = ((), (), s32[]{:S(2)}) async-start(), calls=%async_computation.3 | async-start | bytes 18874368 | tf_op jit(solution)/shard_map/all_gather | solution.py:60
  8.1 5.4 copy-start.3
  106.4 45.1 %copy-start.4 = (f32[512,512]{1,0:T(8,128)}, f32[512,512]{1,0:T(8,128)S(1)}, u32[]{:S(2)}) copy-start(f32[512,512]{1,0:T(8,128)S(1)} %get-tuple-element.206) | copy-start | bytes 3145732
  145.7 5.7 copy-start
  157.9 1.0 copy-start.1
  159.1 2.1 copy-start.7
  159.2 4.8 copy-start.8
  168.6 1.0 copy-start.5
  435.0 8.2 %copy-start.2 = (f32[512,512]{1,0:T(8,128)S(1)}, f32[512,512]{1,0:T(8,128)}, u32[]{:S(2)}) copy-start(f32[512,512]{1,0:T(8,128)} %get-tuple-element.73) | copy-start | bytes 3145732
  435.0 269.6 %all-to-all-start = ((f32[128,2,128,128]{3,2,1,0:T(8,128)}), f32[128,2,128,128]{3,2,1,0:T(8,128)}, u32[]{:S(2)}, u32[]{:S(2)}) async-start(f32[128,2,128,128]{3,2,1,0:T(8,128)} %broadcast_select_fusion), calls=%async_computation | async-start | bytes 33554432 | tf_op jit(solution)/shard_map/all_to_all | solution.py:103
  441.9 50.4 %copy-start.6 = (f32[24,1,1,1,8,512]{5,4,3,2,1,0:T(8,128)S(1)}, f32[24,1,1,1,8,512]{5,4,3,2,1,0:T(8,128)}, u32[]{:S(2)}) copy-start(f32[24,1,1,1,8,512]{5,4,3,2,1,0:T(8,128)} %param.11) | copy-start | bytes 1179652
  441.9 258.9 %all-gather.4.cloned.1.call-start = ((), (), s32[]{:S(2)}) async-start(), calls=%async_computation.1 | async-start | bytes 6684672 | tf_op jit(solution)/shard_map/all_gather | solution.py:47
  495.3 293.3 %all-reduce.3.cloned.1.call-start = ((), (), s32[]{:S(2)}) async-start(), calls=%async_computation.2 | async-start | bytes 2097152 | tf_op jit(solution)/shard_map/psum | solution.py:15
  700.8 1.6 slice-start
Sparse Core Ops, SparseCore 0:
  160.9 188.6 all-gather.5
  703.6 84.9 all-reduce.2
Sparse Core Ops, SparseCore 1:
  495.4 205.4 all-gather.3
where the time goes:
time: 830 us; the launch traced here: 820 us
  waiting for transfers between devices  313 us (38%)
  other arithmetic  309 us (37%)
  local copies, waits for them, and re-layouts  109 us (13%)
  matrix products  60.3 us (7%)
  between operations  21.3 us (3%)
    all_gather x1, waiting for transfers between devices, per_device(): lax.all_gather(solved.reshape(parent_row_blocks, sub_rows, panel_width),...  205 us
    all_gather x1, waiting for transfers between devices, per_device(): everyone = lax.all_gather(leading[None], 'row', axis=0, tiled=True)  89 us
    another operation x14, other arithmetic, per_device(): pivot_lower_factor = jnp.linalg.cholesky(parent_diag)  80.7 us
    another operation x14, other arithmetic, per_device(): child_low = jnp.linalg.cholesky(child_diag[0])  78.9 us
    scatter-add x1, other arithmetic, per_device(): assembled_front.at[target_rows, :, target_cols, :].add(arrived, mode='drop')  51.8 us
    another operation x2, other arithmetic, per_device(): jax.scipy.linalg.solve_triangular(pivot_lower_factor, own_rows.T, lower=T...  40.6 us
    another operation x3, other arithmetic, per_device(): jax.scipy.linalg.solve_triangular(child_low, child_rows.T, lower=True)  39.4 us
    unnamed x24, local copies, waits for them, and re-layouts  28.3 us
  transfers between devices with their start and end apart: 4, of which 3 were waited for; matrix products, arithmetic and copies ran while one was open for 26% of the time, Pallas kernels for 0%

commit v1 on v0

--- a/solution.py
+++ b/solution.py
@@ -12,7 +12,7 @@
 
 def from_root(shard, axis, root):
     mine = lax.axis_index(axis) == root
-    return lax.psum(jnp.where(mine, shard, jnp.zeros_like(shard)), axis)
+    return jnp.sum(lax.all_gather(jnp.where(mine, shard, jnp.zeros_like(shard)), axis), axis=0)
 
 
 def pick_ranked(owners, values, wanted, slot_count, missing):

time: 830 us -> 876 us (1.055)
  the two profiles are of different devices: /device:TPU:0 before, /device:TPU:16 now
where the time goes in v1:
time: 876 us; the launch traced here: 865 us
  waiting for transfers between devices  341 us (39%)
  other arithmetic  318 us (36%)
  local copies, waits for them, and re-layouts  114 us (13%)
  matrix products  64.4 us (7%)
  between operations  19.9 us (2%)
    all_gather x1, waiting for transfers between devices, from_root(): lax.all_gather(jnp.where(mine, shard, jnp.zeros_like(shard)), axis)  325 us
    another operation x14, other arithmetic, per_device(): pivot_lower_factor = jnp.linalg.cholesky(parent_diag)  82.6 us
    another operation x14, other arithmetic, per_device(): child_low = jnp.linalg.cholesky(child_diag[0])  78.6 us
    scatter-add x1, other arithmetic, per_device(): assembled_front.at[target_rows, :, target_cols, :].add(arrived, mode='drop')  51.6 us
    another operation x2, other arithmetic, per_device(): jax.scipy.linalg.solve_triangular(pivot_lower_factor, own_rows.T, lower=T...  44 us
    another operation x3, other arithmetic, per_device(): jax.scipy.linalg.solve_triangular(child_low, child_rows.T, lower=True)  39.4 us
    unnamed x22, local copies, waits for them, and re-layouts  28.9 us
    another operation x24, local copies, waits for them, and re-layouts  22.8 us
  transfers between devices with their start and end apart: 4, of which 2 were waited for; matrix products, arithmetic and copies ran while one was open for 30% of the time, Pallas kernels for 0%

profile of v1, /device:TPU:16, one launch (start us, length us, event | category | flops | bytes accessed | tf_op | source)
XLA Modules:
  0.0 864.7 jit_solution(3214206921580324246)
XLA Ops:
  13.3 11.7 %cholesky.286 = f32[128,128]{1,0:T(8,128)S(1)} custom-call(f32[128,128]{1,0:T(8,128)S(1)} %cholesky.426), custom_call_target="Cholesky" | custom-call | tf_op jit(solution)/shard_map/jit(cholesky)/cholesky | solution.py:56
  25.1 9.8 %custom-call.37 = f32[1,128,128]{1,2,0:T(8,128)S(1)} custom-call(f32[1,128,128]{2,1,0:T(8,128)S(1)} %get-tuple-element.91), custom_call_target="InvertDiagBlocksLowerTriangular" | custom-call | tf_op jit(solution)/shard_map/jit(cholesky)/cholesky | solution.py:56
  35.6 11.7 %cholesky.305 = f32[128,128]{1,0:T(8,128)S(1)} custom-call(f32[128,128]{1,0:T(8,128)S(1)} %cholesky.430), custom_call_target="Cholesky" | custom-call | tf_op jit(solution)/shard_map/jit(cholesky)/cholesky | solution.py:56
  47.4 10.0 %custom-call.38 = f32[1,128,128]{1,2,0:T(8,128)S(1)} custom-call(f32[1,128,128]{2,1,0:T(8,128)S(1)} %get-tuple-element.88), custom_call_target="InvertDiagBlocksLowerTriangular" | custom-call | tf_op jit(solution)/shard_map/jit(cholesky)/cholesky | solution.py:56
  58.0 11.7 %cholesky.326 = f32[128,128]{1,0:T(8,128)S(1)} custom-call(f32[128,128]{1,0:T(8,128)S(1)} %cholesky.435), custom_call_target="Cholesky" | custom-call | tf_op jit(solution)/shard_map/jit(cholesky)/cholesky | solution.py:56
  69.8 9.8 %custom-call.39 = f32[1,128,128]{1,2,0:T(8,128)S(1)} custom-call(f32[1,128,128]{2,1,0:T(8,128)S(1)} %get-tuple-element.85), custom_call_target="InvertDiagBlocksLowerTriangular" | custom-call | tf_op jit(solution)/shard_map/jit(cholesky)/cholesky | solution.py:56
  80.2 11.7 %cholesky.343 = f32[128,128]{1,0:T(8,128)S(1)} custom-call(f32[128,128]{1,0:T(8,128)S(1)} %convolution_subtract_fusion.10), custom_call_target="Cholesky" | custom-call | tf_op jit(solution)/shard_map/jit(cholesky)/cholesky | solution.py:56
  105.6 39.3 %custom-call.28 = f32[4,128,128]{1,2,0:T(8,128)S(1)} custom-call(f32[4,128,128]{2,1,0:T(8,128)S(1)} %get-tuple-element.11), custom_call_target="InvertDiagBlocksLowerTriangular" | custom-call | tf_op jit(solution)/shard_map/jit(_solve_triangular)/triangular_solve | solution.py:58
  165.4 11.7 %cholesky.358 = f32[128,128]{1,0:T(8,128)S(1)} custom-call(f32[128,128]{1,0:T(8,128)S(1)} %cholesky.439), custom_call_target="Cholesky" | custom-call | tf_op jit(solution)/shard_map/jit(cholesky)/cholesky | solution.py:42
  178.3 9.8 %custom-call.40 = f32[1,128,128]{1,2,0:T(8,128)S(1)} custom-call(f32[1,128,128]{2,1,0:T(8,128)S(1)} %get-tuple-element.81), custom_call_target="InvertDiagBlocksLowerTriangular" | custom-call | tf_op jit(solution)/shard_map/jit(cholesky)/cholesky | solution.py:42
  191.3 11.7 %cholesky.377 = f32[128,128]{1,0:T(8,128)S(1)} custom-call(f32[128,128]{1,0:T(8,128)S(1)} %cholesky.443), custom_call_target="Cholesky" | custom-call | tf_op jit(solution)/shard_map/jit(cholesky)/cholesky | solution.py:42
  203.6 10.0 %custom-call.41 = f32[1,128,128]{1,2,0:T(8,128)S(1)} custom-call(f32[1,128,128]{2,1,0:T(8,128)S(1)} %get-tuple-element.78), custom_call_target="InvertDiagBlocksLowerTriangular" | custom-call | tf_op jit(solution)/shard_map/jit(cholesky)/cholesky | solution.py:42
  216.0 11.7 %cholesky.398 = f32[128,128]{1,0:T(8,128)S(1)} custom-call(f32[128,128]{1,0:T(8,128)S(1)} %cholesky.448), custom_call_target="Cholesky" | custom-call | tf_op jit(solution)/shard_map/jit(cholesky)/cholesky | solution.py:42
  241.1 13.2 %cholesky.415 = f32[128,128]{1,0:T(8,128)} custom-call(f32[128,128]{1,0:T(8,128)} %convolution_subtract_fusion.9), custom_call_target="Cholesky" | custom-call | tf_op jit(solution)/shard_map/jit(cholesky)/cholesky | solution.py:42
  264.2 14.4 %while.3 = (s32[]{:T(128)}, f32[512,512]{1,0:T(8,128)}, s32[4,2]{0,1:T(2,128)S(1)}, f32[4,128,128]{2,1,0:T(8,128)}, s32[]{:T(128)}) while((s32[]{:T(128)}, f32[512,512]{1,0:T(8,128)}, s32[4,2]{0,1:T(2,128)S(1)}, f32[4,128,128]{2,1,0:T(8,128)}, s32[]{:T(128)}) %tuple.81), condition=%wide.while_cond.1, body=%wide.while_body.1.sunk | while | flops 2 | bytes 132205 | solution.py:44
  278.6 40.7 %custom-call.29 = f32[4,128,128]{1,2,0:T(8,128)} custom-call(f32[4,128,128]{2,1,0:T(8,128)} %get-tuple-element.19), custom_call_target="InvertDiagBlocksLowerTriangular" | custom-call | tf_op jit(solution)/shard_map/jit(_solve_triangular)/triangular_solve | solution.py:44
  332.0 16.3 %all-gather.8.cloned.1.call-done = f32[8192,512]{0,1:T(8,128)} async-done(((f32[1024,512]{0,1:T(8,128)}), f32[8192,512]{0,1:T(8,128)}) %all-gather.8.cloned.1.call-update) | async-done | bytes 16777232 | tf_op jit(solution)/shard_map/all_gather | solution.py:60
  348.3 21.2 %copy.78 = f32[64,8,8,1024]{3,2,1,0:T(8,128)} copy(f32[64,8,8,1024]{3,1,2,0:T(8,128)} %bitcast.227) | data formatting | bytes 33554432
  379.2 20.6 %fusion = f32[256,8,8,128]{3,1,2,0:T(8,128)S(1)} fusion(f32[256,8,8,128]{3,2,1,0:T(8,128)} %bitcast.235, f32[128,2048]{1,0:T(8,128)} %copy-done.1, f32[128,2048]{1,0:T(8,128)S(1)} %fusion.56, f32[128,2048]{1,0:T(8,128)S(1)} %fusion.58, f32[128,2048]{1,0:T(8,128)S(1)} %fusion.16, f32[1,1024,512]{1,0,2:T(1,128)} %constant_dynamic-slice_fusion.2), kind=kOutput, calls=%fused_computation.7 | convolution fusion | flops 12890144768 | bytes 23068672 | tf_op jit(solution)/shard_map/dot_general | solution.py:62
  406.6 16.0 %gather_fusion = f32[256,128,128]{2,1,0:T(8,128)} fusion(f32[16,128,8,128]{3,1,2,0:T(8,128)} %copy.67, s32[256]{0:T(256)S(1)} %reshape.584), kind=kCustom, calls=%fused_computation | custom fusion | bytes 33556480 | tf_op jit(solution)/shard_map/gather | solution.py:102
  422.6 11.4 %broadcast_select_fusion = f32[128,2,128,128]{3,2,1,0:T(8,128)} fusion(f32[128,2,128,128]{3,2,1,0:T(8,128)} %bitcast.223, pred[128,2]{1,0:T(8,128)(4,1)S(1)} %bitcast.243), kind=kLoop, calls=%fused_computation.9 | loop fusion | flops 4194304 | bytes 33554688 | tf_op jit(solution)/shard_map/select_n | solution.py:102
  444.7 324.6 %all-gather.10.cloned.1.call-done = f32[32,1,128,512]{3,2,1,0:T(8,128)} async-done(((f32[4,1,128,512]{3,2,1,0:T(8,128)}), f32[32,1,128,512]{3,2,1,0:T(8,128)}) %all-gather.10.cloned.1.call-update) | async-done | bytes 8388624 | tf_op jit(solution)/shard_map/all_gather | solution.py:15
  777.3 51.6 %scatter_fusion = f32[24,128,4,128]{3,1,2,0:T(8,128)} fusion(f32[24,128,4,128]{3,1,2,0:T(8,128)} %broadcast_in_dim.109, s32[256]{0:T(256)S(1)} %reshape.592, f32[256,128,128]{2,1,0:T(8,128)} %bitcast.23), kind=kCustom, calls=%fused_computation.1 | custom fusion | flops 4194304 | bytes 50333696 | tf_op jit(solution)/shard_map/scatter-add | solution.py:113
  836.7 13.4 %bitcast_subtract_fusion.1 = f32[3072,512]{1,0:T(8,128)} fusion(f32[384,8,4,128]{3,2,1,0:T(4,128)S(1)} %bitcast.225, f32[3072,512]{1,0:T(8,128)} %bitcast.232, f32[512,512]{1,0:T(8,128)S(1)} %bitcast.237), kind=kOutput, calls=%fused_computation.10 | convolution fusion | flops 9665249280 | bytes 19922944 | tf_op jit(solution)/shard_map/dot_general | solution.py:117
  (173 shorter events, 153.5 us)
Async XLA Ops:
  7.2 341.1 %all-gather.8.cloned.1.call-start = ((), (), s32[]{:S(2)}) async-start(), calls=%async_computation.2 | async-start | bytes 18874368 | tf_op jit(solution)/shard_map/all_gather | solution.py:60
  7.2 5.4 copy-start.2
  105.6 45.1 %copy-start.3 = (f32[512,512]{1,0:T(8,128)}, f32[512,512]{1,0:T(8,128)S(1)}, u32[]{:S(2)}) copy-start(f32[512,512]{1,0:T(8,128)S(1)} %get-tuple-element.205) | copy-start | bytes 3145732
  144.9 5.7 copy-start
  157.0 1.0 copy-start.1
  159.9 280.6 %all-gather.6.cloned.1.call-start = ((), (), s32[]{:S(2)}) async-start(), calls=%async_computation.1 | async-start | bytes 6684672 | tf_op jit(solution)/shard_map/all_gather | solution.py:47
  164.4 1.0 copy-start.4
  239.0 80.3 %copy-start.5 = (f32[24,1,1,1,8,512]{5,4,3,2,1,0:T(8,128)S(1)}, f32[24,1,1,1,8,512]{5,4,3,2,1,0:T(8,128)}, u32[]{:S(2)}) copy-start(f32[24,1,1,1,8,512]{5,4,3,2,1,0:T(8,128)} %param.11) | copy-start | bytes 1179652
  260.3 68.7 %copy-start.6 = (s32[2,128]{1,0:T(2,128)S(1)}, s32[2,128]{1,0:T(2,128)}, u32[]{:S(2)}) copy-start(s32[2,128]{1,0:T(2,128)} %param.12) | copy-start | bytes 3076
  260.3 71.4 %copy-start.7 = (s32[2]{0:T(128)S(1)}, s32[2]{0:T(128)}, u32[]{:S(2)}) copy-start(s32[2]{0:T(128)} %constant.261.clone.1) | copy-start | bytes 28
  433.9 339.9 %all-to-all-start = ((f32[128,2,128,128]{3,2,1,0:T(8,128)}), f32[128,2,128,128]{3,2,1,0:T(8,128)}, u32[]{:S(2)}, u32[]{:S(2)}) async-start(f32[128,2,128,128]{3,2,1,0:T(8,128)} %broadcast_select_fusion), calls=%async_computation | async-start | bytes 33554432 | tf_op jit(solution)/shard_map/all_to_all | solution.py:103
  440.4 328.9 %all-gather.10.cloned.1.call-start = ((), (), s32[]{:S(2)}) async-start(), calls=%async_computation.3 | async-start | bytes 9437184 | tf_op jit(solution)/shard_map/all_gather | solution.py:15
  440.5 1.6 slice-start
Sparse Core Ops, SparseCore 0:
  160.0 188.1 all-gather.7
  350.0 39.7 all-gather.5
  444.1 325.0 all-gather.9
